TPU v7x, 512 devices: a whole 4x8x8 slice. The times are simulated.
512 devices in a mesh: dp: 4 (over y_hi, core), context: 16 (over y_lo, x), tensor: 8 (over z).
Axes of the slice: x: 4, y: 8 (y_hi: 2, y_lo: 4; y = y_hi * 4 + y_lo), z: 8, core: 2. Of those that a mesh axis runs over, the one named last changes fastest.
Arguments:
- queries: bfloat16 [8192, 4096], P(('dp', 'context'), 'tensor'), parts along dimension 0, may hold values from -6 to 6
- keys: bfloat16 [8192, 1024], P(('dp', 'context'), 'tensor'), parts along dimension 0, may hold values from -6 to 6
- values: bfloat16 [8192, 1024], P(('dp', 'context'), 'tensor'), parts along dimension 0, may hold values from -6 to 6
- order: int32 [8192], P('dp'), parts along dimension 0, may hold values from 0 to 2047, as said below
- out_weight: bfloat16 [4096, 4096], P('tensor', 'context'), may hold values from -0.125 to 0.125
Outputs:
- output: bfloat16 [8192, 4096], P(('dp', 'context'), 'tensor'), parts along dimension 0
There are 4 independent parts, one for each index of `dp`. A program takes and returns all parts, laid end to end along the dimension named above; an argument that names none is the same for every part. Nothing has to cross between parts.
Inputs may be any that keep to these rules, and one draw needn't show every extreme that they name: A permutation of the positions; each aligned block of 128 rows holds 128 consecutive positions in increasing order, starting at a multiple of 128.
All inputs are finite; a program needn't handle non-finite values.
Results may differ from a plain program's by a relative error of at most 0.019.
Values may be sent and summed in bfloat16 or wider, within the bound.
No kernel may reach another device: no remote copies, remote signals or barrier semaphores. Data moves between devices by JAX's collectives and lax.ppermute only.
A program may use at most 64 MiB of HBM per device.

v0:
```python
import math
import jax
import jax.numpy as jnp
from jax import lax
from jax.sharding import PartitionSpec as P

QUERY_HEADS = 32
KEY_VALUE_HEADS = 8
HEAD_SIZE = 128


def per_device(queries, keys, values, order, out_weight):
    row_count = queries.shape[0]
    local_groups = keys.shape[1] // HEAD_SIZE
    query_head_group = QUERY_HEADS // KEY_VALUE_HEADS
    score_scale = 1.0 / math.sqrt(HEAD_SIZE)
    first_row = lax.axis_index("context") * row_count
    query_pos = lax.dynamic_slice_in_dim(order, first_row, row_count, 0)
    stacked = queries.reshape(row_count, local_groups, query_head_group, HEAD_SIZE)
    stacked = stacked.transpose(1, 2, 0, 3).reshape(
        local_groups, query_head_group * row_count, HEAD_SIZE
    )
    stacked_pos = jnp.tile(query_pos, query_head_group)
    stacked_rows = query_head_group * row_count
    kv_part = lax.all_gather(jnp.concatenate([keys, values], axis=1), "context", axis=0, tiled=True)
    key_part = kv_part[:, : keys.shape[1]]
    value_part = kv_part[:, keys.shape[1] :]
    key_count = key_part.shape[0]
    running_max = jnp.full((local_groups, stacked_rows), -1e30, jnp.float32)
    key_heads = key_part.reshape(key_count, local_groups, HEAD_SIZE)
    value_heads = value_part.reshape(key_count, local_groups, HEAD_SIZE)
    scores = (
        jnp.einsum("grd,kgd->grk", stacked, key_heads, preferred_element_type=jnp.float32)
        * score_scale
    )
    visible = order[None, None, :] <= stacked_pos[None, :, None]
    scores = jnp.where(visible, scores, -1e30)
    new_max = jnp.maximum(running_max, jnp.max(scores, axis=2))
    weights = jnp.where(visible, jnp.exp(scores - new_max[..., None]), 0.0)
    new_sum = jnp.sum(weights, axis=2)
    product = jnp.einsum(
        "grk,kgd->grd",
        weights.astype(jnp.bfloat16),
        value_heads,
        preferred_element_type=jnp.float32,
    )
    attended = (product / new_sum[..., None]).astype(jnp.bfloat16)
    attended = attended.reshape(local_groups, query_head_group, row_count, HEAD_SIZE).transpose(
        2, 0, 1, 3
    )
    attended = attended.reshape(row_count, local_groups * query_head_group * HEAD_SIZE)
    partial_out = jnp.dot(
        attended,
        lax.all_gather(out_weight, "context", axis=1, tiled=True),
        preferred_element_type=jnp.float32,
    )
    return lax.psum_scatter(
        partial_out.astype(jnp.bfloat16), "tensor", scatter_dimension=1, tiled=True
    )


def solution(mesh):
    placed = (
        P(("dp", "context"), "tensor"),
        P(("dp", "context"), "tensor"),
        P(("dp", "context"), "tensor"),
        P("dp"),
        P("tensor", "context"),
    )
    return jax.shard_map(
        per_device,
        mesh=mesh,
        in_specs=placed,
        out_specs=P(("dp", "context"), "tensor"),
        check_vma=False,
    )
```

profile of v0, /device:TPU:6, one launch (start us, length us, event | category | flops | bytes accessed | tf_op | source)
XLA Modules:
  0.0 242.8 jit_solution(16070495082497380029)
XLA Ops:
  6.5 0.0 copy-start
  6.5 0.0 all-gather.3.cloned.1.call-start
  6.5 1.4 pad_maximum_fusion
  8.0 0.0 all-gather.3.cloned.1.call-update
  8.0 0.0 all-gather.5.cloned.1.call-start
  8.0 0.7 all-gather.5.cloned.1.call-update
  8.7 0.0 reduce-scatter.2.cloned.1.call-start
  8.8 1.0 copy.7
  9.8 0.1 copy.8
  10.0 0.8 dynamic_slice.3
  10.7 82.1 %all-gather.3.cloned.1.call-done = bf16[2048,256]{1,0:T(8,128)(2,1)} async-done(((bf16[128,256]{1,0:T(8,128)(2,1)}), bf16[2048,256]{1,0:T(8,128)(2,1)}) %all-gather.3.cloned.1.call-update) | async-done | bytes 1048592 | tf_op jit(solution)/shard_map/all_gather | solution.py:25
  92.9 0.0 copy-start.1
  92.9 2.0 fusion
  94.9 0.0 copy-done
  94.9 1.3 fusion.1
  96.1 0.0 copy-done.1
  96.2 1.6 fusion.8
  97.8 0.1 copy.9
  97.9 92.8 %all-gather.5.cloned.1.call-done = bf16[512,4096]{1,0:T(8,128)(2,1)} async-done(((bf16[512,256]{1,0:T(8,128)(2,1)}), bf16[512,4096]{1,0:T(8,128)(2,1)}) %all-gather.5.cloned.1.call-update) | async-done | bytes 4194320 | tf_op jit(solution)/shard_map/all_gather | solution.py:54
  190.7 3.9 %convolution_convert_fusion = bf16[128,4096]{1,0:T(8,128)(2,1)} fusion(bf16[128,512]{0,1:T(8,128)(2,1)S(1)} %bitcast.29, bf16[512,4096]{1,0:T(8,128)(2,1)} %all-gather.5.cloned.1.call-done), kind=kOutput, calls=%fused_computation.2 | convolution fusion | flops 537395200 | bytes 5373952 | tf_op jit(solution)/shard_map/dot_general | solution.py:52
  194.6 0.0 reduce-scatter.2.cloned.1.call-update
  194.6 41.6 %reduce-scatter.2.cloned.1.call-done = bf16[128,512]{1,0:T(8,128)(2,1)} async-done(((bf16[128,4096]{1,0:T(8,128)(2,1)}), bf16[128,512]{1,0:T(8,128)(2,1)}) %reduce-scatter.2.cloned.1.call-update) | async-done | bytes 131088 | tf_op jit(solution)/shard_map/reduce_scatter | solution.py:57
  (2 shorter events, 0.0 us)
Async XLA Ops:
  6.5 88.3 %copy-start = (s32[2048]{0:T(1024)S(1)}, s32[2048]{0:T(1024)}, u32[]{:S(2)}) copy-start(s32[2048]{0:T(1024)} %param.8) | copy-start | bytes 24580
  6.5 86.3 %all-gather.3.cloned.1.call-start = ((), (), s32[]{:S(2)}) async-start(), calls=%async_computation.1 | async-start | bytes 1114112 | tf_op jit(solution)/shard_map/all_gather | solution.py:25
  8.0 182.7 %all-gather.5.cloned.1.call-start = ((), (), s32[]{:S(2)}) async-start(), calls=%async_computation.2 | async-start | bytes 4456448 | tf_op jit(solution)/shard_map/all_gather | solution.py:54
  8.7 227.5 %reduce-scatter.2.cloned.1.call-start = ((), (), s32[]{:S(2)}) async-start(), calls=%async_computation.3 | async-start | bytes 1179648 | tf_op jit(solution)/shard_map/reduce_scatter | solution.py:57
  92.9 3.3 %copy-start.1 = (bf16[2048,256]{1,0:T(8,128)(2,1)S(1)}, bf16[2048,256]{1,0:T(8,128)(2,1)}, u32[]{:S(2)}) copy-start(bf16[2048,256]{1,0:T(8,128)(2,1)} %all-gather.3.cloned.1.call-done) | copy-start | bytes 3145732
Sparse Core Ops, SparseCore 0:
  9.4 83.3 all-gather.2
  94.9 95.7 all-gather.4
  194.8 41.4 reduce-scatter.1
where the time goes:
time: 243 us
  waiting for transfers between devices  217 us (89%)
  between operations  13.2 us (5%)
  matrix products  7.49 us (3%)
  other arithmetic  2.69 us (1%)
    all_gather x1, waiting for transfers between devices, per_device(): lax.all_gather(out_weight, 'context', axis=1, tiled=True)  92.8 us
    all_gather x1, waiting for transfers between devices, per_device(): lax.all_gather(jnp.concatenate([keys, values], axis=1), 'context', axis=0...  82.1 us
    reduce_scatter x1, waiting for transfers between devices, per_device(): lax.psum_scatter(partial_out.astype(jnp.bfloat16), 'tensor', scatter_dime...  41.6 us
  transfers between devices with their start and end apart: 3, of which 3 were waited for; matrix products, arithmetic and copies ran while one was open for 3% of the time, Pallas kernels for 0%

commit v1 on v0

--- a/solution.py
+++ b/solution.py
@@ -22,7 +22,15 @@
     )
     stacked_pos = jnp.tile(query_pos, query_head_group)
     stacked_rows = query_head_group * row_count
-    kv_part = lax.all_gather(jnp.concatenate([keys, values], axis=1), "context", axis=0, tiled=True)
+    kv_part = jnp.concatenate(
+        lax.all_to_all(
+            jnp.stack([jnp.concatenate([keys, values], axis=1)] * lax.axis_size("context")),
+            "context",
+            0,
+            0,
+        ),
+        axis=0,
+    )
     key_part = kv_part[:, : keys.shape[1]]
     value_part = kv_part[:, keys.shape[1] :]
     key_count = key_part.shape[0]

time: 243 us -> 170 us (0.70)
  waiting for transfers between devices: 217 us -> 135 us
  starting transfers between devices: 0.08 us -> 9.45 us
    all_gather x1 -> x0, waiting for transfers between devices: 82.1 us -> none  [per_device(): lax.all_gather(jnp.concatenate([keys, values], axis=1), 'context', axis=0...]
    all_gather x1, waiting for transfers between devices: 92.8 us -> 65.2 us  [per_device(): lax.all_gather(out_weight, 'context', axis=1, tiled=True)]
    all_to_all x0 -> x1, waiting for transfers between devices: none -> 23.6 us  [per_device(): lax.all_to_all(jnp.stack([jnp.concatenate([keys, values], axis=1)] * lax....]
    all_to_all x0 -> x1, starting transfers between devices: none -> 9.41 us  [per_device(): lax.all_to_all(jnp.stack([jnp.concatenate([keys, values], axis=1)] * lax....]
    reduce_scatter x1, waiting for transfers between devices: 41.6 us -> 45.2 us  [per_device(): lax.psum_scatter(partial_out.astype(jnp.bfloat16), 'tensor', scatter_dime...]
  transfers between devices with their start and end apart: 3 -> 3, of which waited for: 3 -> 3; matrix products, arithmetic and copies ran while one was open for 3% -> 5% of each run, Pallas kernels for 0% -> 0%
where the time goes in v1:
time: 170 us
  waiting for transfers between devices  135 us (79%)
  between operations  13.4 us (8%)
  starting transfers between devices  9.45 us (6%)
  matrix products  6.92 us (4%)
  local copies, waits for them, and re-layouts  3.13 us (2%)
  other arithmetic  2.05 us (1%)
    all_gather x1, waiting for transfers between devices, per_device(): lax.all_gather(out_weight, 'context', axis=1, tiled=True)  65.2 us
    reduce_scatter x1, waiting for transfers between devices, per_device(): lax.psum_scatter(partial_out.astype(jnp.bfloat16), 'tensor', scatter_dime...  45.2 us
    all_to_all x1, waiting for transfers between devices, per_device(): lax.all_to_all(jnp.stack([jnp.concatenate([keys, values], axis=1)] * lax....  23.6 us
    all_to_all x1, starting transfers between devices, per_device(): lax.all_to_all(jnp.stack([jnp.concatenate([keys, values], axis=1)] * lax....  9.41 us
    dot_general x1, matrix products, per_device(): jnp.dot(attended, lax.all_gather(out_weight, 'context', axis=1, tiled=Tru...  3.9 us
  transfers between devices with their start and end apart: 3, of which 3 were waited for; matrix products, arithmetic and copies ran while one was open for 5% of the time, Pallas kernels for 0%

profile of v1, /device:TPU:6, one launch (start us, length us, event | category | flops | bytes accessed | tf_op | source)
XLA Modules:
  0.0 169.7 jit_solution(1522206891832039284)
XLA Ops:
  6.5 0.0 all-gather.2.cloned.1.call-start
  6.5 0.7 all-gather.2.cloned.1.call-update
  7.3 0.8 pad_maximum_fusion
  8.0 1.1 stack.2
  9.1 0.0 copy-start
  9.1 9.4 %all-to-all-start = ((bf16[16,128,256]{2,1,0:T(8,128)(2,1)}), bf16[16,128,256]{2,1,0:T(8,128)(2,1)S(1)}, u32[]{:S(2)}, u32[]{:S(2)}) async-start(bf16[16,128,256]{2,1,0:T(8,128)(2,1)} %stack.2), calls=%async_computation | async-start | bytes 2097152 | tf_op jit(solution)/shard_map/all_to_all | solution.py:26
  18.5 0.0 reduce-scatter.2.cloned.1.call-start
  18.6 1.0 copy.7
  19.6 0.1 copy.8
  19.7 0.8 dynamic_slice.3
  20.5 23.6 %all-to-all-done = bf16[16,128,256]{2,1,0:T(8,128)(2,1)S(1)} async-done(((bf16[16,128,256]{2,1,0:T(8,128)(2,1)}), bf16[16,128,256]{2,1,0:T(8,128)(2,1)S(1)}, u32[]{:S(2)}, u32[]{:S(2)}) %all-to-all-start) | async-done | bytes 1048608 | tf_op jit(solution)/shard_map/all_to_all | solution.py:26
  44.1 1.4 fusion
  45.6 0.0 copy-done
  45.6 1.3 fusion.1
  46.8 1.6 fusion.8
  48.4 0.1 copy.9
  48.6 65.2 %all-gather.2.cloned.1.call-done = bf16[512,4096]{1,0:T(8,128)(2,1)} async-done(((bf16[512,256]{1,0:T(8,128)(2,1)}), bf16[512,4096]{1,0:T(8,128)(2,1)}) %all-gather.2.cloned.1.call-update) | async-done | bytes 4194320 | tf_op jit(solution)/shard_map/all_gather | solution.py:62
  113.7 3.9 %convolution_convert_fusion = bf16[128,4096]{1,0:T(8,128)(2,1)} fusion(bf16[128,512]{0,1:T(8,128)(2,1)S(1)} %bitcast.32, bf16[512,4096]{1,0:T(8,128)(2,1)} %all-gather.2.cloned.1.call-done), kind=kOutput, calls=%fused_computation.2 | convolution fusion | flops 537395200 | bytes 5373952 | tf_op jit(solution)/shard_map/dot_general | solution.py:60
  117.6 0.0 reduce-scatter.2.cloned.1.call-update
  117.7 45.2 %reduce-scatter.2.cloned.1.call-done = bf16[128,512]{1,0:T(8,128)(2,1)} async-done(((bf16[128,4096]{1,0:T(8,128)(2,1)}), bf16[128,512]{1,0:T(8,128)(2,1)}) %reduce-scatter.2.cloned.1.call-update) | async-done | bytes 131088 | tf_op jit(solution)/shard_map/reduce_scatter | solution.py:65
  (2 shorter events, 0.0 us)
Async XLA Ops:
  6.5 107.2 %all-gather.2.cloned.1.call-start = ((), (), s32[]{:S(2)}) async-start(), calls=%async_computation.2 | async-start | bytes 4456448 | tf_op jit(solution)/shard_map/all_gather | solution.py:62
  9.1 36.4 %copy-start = (s32[2048]{0:T(1024)S(1)}, s32[2048]{0:T(1024)}, u32[]{:S(2)}) copy-start(s32[2048]{0:T(1024)} %param.8) | copy-start | bytes 24580
  9.1 35.0 %all-to-all-start = ((bf16[16,128,256]{2,1,0:T(8,128)(2,1)}), bf16[16,128,256]{2,1,0:T(8,128)(2,1)S(1)}, u32[]{:S(2)}, u32[]{:S(2)}) async-start(bf16[16,128,256]{2,1,0:T(8,128)(2,1)} %stack.2), calls=%async_computation | async-start | bytes 2097152 | tf_op jit(solution)/shard_map/all_to_all | solution.py:26
  18.5 144.4 %reduce-scatter.2.cloned.1.call-start = ((), (), s32[]{:S(2)}) async-start(), calls=%async_computation.3 | async-start | bytes 1179648 | tf_op jit(solution)/shard_map/reduce_scatter | solution.py:65
Sparse Core Ops, SparseCore 0:
  9.3 104.3 all-gather.1
  117.8 45.0 reduce-scatter.1
